TPU v7x, 512 devices: a whole 4x8x8 slice. The times are simulated.
512 devices in a mesh: grp: 4 (over x), gx: 16 (over z_hi, y), gy: 8 (over z_lo, core).
Axes of the slice: x: 4, y: 8, z: 8 (z_hi: 2, z_lo: 4; z = z_hi * 4 + z_lo), core: 2. Of those that a mesh axis runs over, the one named last changes fastest.
Arguments:
- fwd_now: float32 [3, 64, 64, 128], P(None, 'gx', 'gy'), may hold values from -6 to 6
- fwd_prev: float32 [3, 64, 64, 128], P(None, 'gx', 'gy'), may hold values from -6 to 6
- adj_now: float32 [16, 3, 64, 64, 128], P('grp', None, 'gx', 'gy'), may hold values from -6 to 6
- adj_prev: float32 [16, 3, 64, 64, 128], P('grp', None, 'gx', 'gy'), may hold values from -6 to 6
- lame_first: float32 [64, 64, 128], P('gx', 'gy'), may hold values from 0.5 to 2
- shear_mod: float32 [64, 64, 128], P('gx', 'gy'), may hold values from 0.3 to 1.2
- buoyancy: float32 [64, 64, 128], P('gx', 'gy'), may hold values from 0.5 to 1
- master_cell: int32 [1], replicated, may hold values from 0 to 524287
- master_lag: int32 [1], replicated, may hold values from 0 to 254
- master_trace: float32 [256, 3], replicated, may hold values from -96 to 96
- receiver_cell: int32 [16], P('grp'), may hold values from 0 to 524287
- receiver_lag: int32 [16], P('grp'), may hold values from 0 to 254
- receiver_trace: float32 [16, 256, 3], P('grp'), may hold values from -96 to 96
Outputs:
- adj_final: float32 [16, 3, 64, 64, 128], P('grp', None, 'gx', 'gy')
- kernels: float32 [2, 64, 64, 128], P(None, 'gx', 'gy', 'grp')
Inputs may be any that keep to these rules, and one draw needn't show every extreme that they name: `receiver_cell`: cell index in the whole grid, numbered (x * 64 + y) * 128 + z. `master_cell`: cell index in the whole grid, numbered (x * 64 + y) * 128 + z.
All inputs are finite; a program needn't handle non-finite values.
Results may differ from a plain program's by a relative error of at most 0.00011.
Values sent between devices are 32-bit elements; how exact they have to be, the bound alone decides.
No kernel may reach another device: no remote copies, remote signals or barrier semaphores. Data moves between devices by JAX's collectives and lax.ppermute only.
A program may use at most 64 MiB of HBM per device.

v0:
```python
import jax
import jax.numpy as jnp
from jax import lax
from jax.sharding import PartitionSpec as P

STEPS = 2
time_step_sq = 0.0625


def with_halo(cells, sides, width):
    for axis, dim in sides:
        count = lax.axis_size(axis)
        ends = count - 1
        head = lax.slice_in_dim(cells, 0, width, axis=dim)
        tail = lax.slice_in_dim(cells, cells.shape[dim] - width, cells.shape[dim], axis=dim)
        cells = jnp.concatenate(
            [
                lax.ppermute(tail, axis, [(i, (i + 1) % count) for i in range(ends)]),
                cells,
                lax.ppermute(head, axis, [((i + 1) % count, i) for i in range(ends)]),
            ],
            axis=dim,
        )
    return cells


def passed_along(value, axis, by):
    size = lax.axis_size(axis)
    pairs = [(i, i + by) for i in range(size) if 0 <= i + by < size]
    return lax.ppermute(value, axis, pairs)


def backward_diff(stress, axis):
    upper = stress[:, 1:, 1:, 1:]
    if axis == 1:
        lower = stress[:, :-1, 1:, 1:]
    elif axis == 2:
        lower = stress[:, 1:, :-1, 1:]
    else:
        lower = stress[:, 1:, 1:, :-1]
    return upper - lower


def stencil(padded, lame_pad, shear_pad):
    span_x = padded.shape[2] - 2
    span_y = padded.shape[3] - 2
    span_z = padded.shape[4] - 2
    anchor = padded[:, :, : span_x + 1, : span_y + 1, : span_z + 1]
    grad_x = padded[:, :, 1:, : span_y + 1, : span_z + 1] - anchor
    grad_y = padded[:, :, : span_x + 1, 1:, : span_z + 1] - anchor
    grad_z = padded[:, :, : span_x + 1, : span_y + 1, 1:] - anchor
    strain_xx = grad_x[:, 0]
    strain_yy = grad_y[:, 1]
    strain_zz = grad_z[:, 2]
    strain_xy = 0.5 * (grad_y[:, 0] + grad_x[:, 1])
    strain_xz = 0.5 * (grad_z[:, 0] + grad_x[:, 2])
    strain_yz = 0.5 * (grad_z[:, 1] + grad_y[:, 2])
    lame = lame_pad[: span_x + 1, : span_y + 1, : span_z + 1]
    shear = shear_pad[: span_x + 1, : span_y + 1, : span_z + 1]
    dilation = strain_xx + strain_yy + strain_zz
    stress_xx = lame * dilation + 2.0 * shear * strain_xx
    stress_yy = lame * dilation + 2.0 * shear * strain_yy
    stress_zz = lame * dilation + 2.0 * shear * strain_zz
    stress_xy = 2.0 * shear * strain_xy
    stress_xz = 2.0 * shear * strain_xz
    stress_yz = 2.0 * shear * strain_yz
    force_x = (
        backward_diff(stress_xx, 1) + backward_diff(stress_xy, 2) + backward_diff(stress_xz, 3)
    )
    force_y = (
        backward_diff(stress_xy, 1) + backward_diff(stress_yy, 2) + backward_diff(stress_yz, 3)
    )
    force_z = (
        backward_diff(stress_xz, 1) + backward_diff(stress_yz, 2) + backward_diff(stress_zz, 3)
    )
    force = jnp.stack([force_x, force_y, force_z], axis=1)
    strain = jnp.stack([strain_xx, strain_yy, strain_zz, strain_xy, strain_xz, strain_yz], axis=1)
    return (force, strain[:, :, 1:, 1:, 1:])


def faces(fields):
    count = fields.shape[0]
    flat = fields.reshape((count * 3,) + fields.shape[2:])
    grown = with_halo(flat, (("gx", 1), ("gy", 2)), 1)
    grown = jnp.pad(grown, ((0, 0), (0, 0), (0, 0), (1, 1)))
    return grown.reshape((count, 3) + grown.shape[1:])


def lower_rims(moduli):
    pairs, cells_x, cells_y, depth = moduli.shape
    from_x = passed_along(moduli[:, cells_x - 1 :], "gx", 1)
    from_y = passed_along(moduli[:, :, cells_y - 1 :], "gy", 1)
    corner = jnp.zeros((pairs, 1, 1, depth), jnp.float32)
    top_row = jnp.concatenate([corner, from_y], axis=1)
    rest = jnp.concatenate([from_x, moduli], axis=1)
    grown = jnp.concatenate([top_row, rest], axis=2)
    return jnp.pad(grown, ((0, 0), (0, 1), (0, 1), (1, 1)))


def locate(cells, start_x, start_y, start_z, width_y, depth, span_x, span_y, span_z):
    coord_x = cells // (width_y * depth) - start_x
    coord_y = cells // depth % width_y - start_y
    coord_z = cells % depth - start_z
    index_x = lax.broadcasted_iota(jnp.int32, (1, span_x, 1, 1), 1)
    index_y = lax.broadcasted_iota(jnp.int32, (1, 1, span_y, 1), 2)
    index_z = lax.broadcasted_iota(jnp.int32, (1, 1, 1, span_z), 3)
    found = (
        (index_x == coord_x[:, None, None, None])
        & (index_y == coord_y[:, None, None, None])
        & (index_z == coord_z[:, None, None, None])
    )
    return found.astype(jnp.float32)


def pick(trace, lags):
    positions = lax.broadcasted_iota(jnp.int32, (1, trace.shape[1]), 1)
    chosen = positions == lags[:, None]
    return jnp.sum(jnp.where(chosen[:, :, None], trace, 0.0), axis=1)


def advance(current, earlier, force, amplitudes, masks, buoyancy):
    source = amplitudes[:, :, None, None, None] * masks[:, None]
    return 2.0 * current - earlier + time_step_sq * buoyancy * (force + source)


def correlate(master, strains, totals):
    weights = jnp.array([1.0, 1.0, 1.0, 2.0, 2.0, 2.0], jnp.float32)[:, None, None, None]
    summed = jnp.sum(strains, axis=0)
    dilation_term = (master[0] + master[1] + master[2]) * (summed[0] + summed[1] + summed[2])
    shear_term = 2.0 * jnp.sum(weights * master * summed, axis=0)
    return totals + jnp.stack([dilation_term, shear_term])


def local(
    fwd_now,
    fwd_prev,
    adj_now,
    adj_prev,
    lame_first,
    shear_mod,
    buoyancy,
    master_cell,
    master_lag,
    master_trace,
    receiver_cell,
    receiver_lag,
    receiver_trace,
):
    cells_x, cells_y, depth = lame_first.shape
    groups = lax.axis_size("grp")
    receivers = adj_now.shape[0]
    width_y = cells_y * lax.axis_size("gy")
    start_x = lax.axis_index("gx") * cells_x
    start_y = lax.axis_index("gy") * cells_y
    moduli = lower_rims(jnp.stack([lame_first, shear_mod]))
    lame_pad = moduli[0]
    shear_pad = moduli[1]
    receiver_masks = locate(
        receiver_cell, start_x, start_y, 0, width_y, depth, cells_x, cells_y, depth
    )
    receiver_amps = [pick(receiver_trace, receiver_lag + instant) for instant in range(STEPS)]
    master_amps = [pick(master_trace[None], master_lag + instant) for instant in range(STEPS)]
    totals = jnp.zeros((2, cells_x, cells_y, depth), jnp.float32)
    share = depth // groups
    z_start = lax.axis_index("grp") * share
    master_now = lax.dynamic_slice_in_dim(fwd_now, z_start, share, 3)
    master_prev = lax.dynamic_slice_in_dim(fwd_prev, z_start, share, 3)
    lame_share = lax.dynamic_slice_in_dim(lame_pad, z_start, share + 2, 2)
    shear_share = lax.dynamic_slice_in_dim(shear_pad, z_start, share + 2, 2)
    buoyancy_share = lax.dynamic_slice_in_dim(buoyancy, z_start, share, 2)
    master_mask = locate(
        master_cell, start_x, start_y, z_start, width_y, depth, cells_x, cells_y, share
    )
    adjoint = adj_now
    adjoint_prev = adj_prev
    for instant in range(STEPS):
        grown = with_halo(master_now, (("grp", 3), ("gx", 1), ("gy", 2)), 1)
        master_force, master_strain = stencil(grown[None], lame_share, shear_share)
        master_whole = lax.all_gather(master_strain[0], "grp", axis=3, tiled=True)
        if instant + 1 < STEPS:
            master_next = advance(
                master_now[None],
                master_prev[None],
                master_force,
                master_amps[instant],
                master_mask,
                buoyancy_share,
            )[0]
            master_prev, master_now = (master_now, master_next)
        padded = faces(adjoint)
        force, strain = stencil(padded, lame_pad, shear_pad)
        totals = correlate(master_whole, strain, totals)
        adjoint_next = advance(
            adjoint, adjoint_prev, force, receiver_amps[instant], receiver_masks, buoyancy
        )
        adjoint_prev, adjoint = (adjoint, adjoint_next)
    scale_out = 1.0 / (STEPS * receivers * groups)
    kernels = lax.psum_scatter(totals * scale_out, "grp", scatter_dimension=3, tiled=True)
    return (adjoint, kernels)


def solution(mesh):
    in_specs = (
        P(None, "gx", "gy", None),
        P(None, "gx", "gy", None),
        P("grp", None, "gx", "gy", None),
        P("grp", None, "gx", "gy", None),
        P("gx", "gy", None),
        P("gx", "gy", None),
        P("gx", "gy", None),
        P(),
        P(),
        P(),
        P("grp"),
        P("grp"),
        P("grp", None, None),
    )
    out_specs = (P("grp", None, "gx", "gy", None), P(None, "gx", "gy", "grp"))
    return jax.shard_map(local, mesh=mesh, in_specs=in_specs, out_specs=out_specs, check_vma=False)
```

profile of v0, /device:TPU:8, one launch (start us, length us, event | category | flops | bytes accessed | tf_op | source)
XLA Modules:
  0.0 201.1 jit_solution(10094206814735372614)
XLA Ops:
  7.2 0.7 copy_bitcast_fusion
  8.0 1.7 collective-permute-start
  9.7 3.5 %collective-permute-start.1 = (f32[2,1,8,128]{3,1,2,0:T(1,128)S(1)}, f32[2,1,8,128]{3,1,2,0:T(1,128)S(1)}, u32[]{:S(2)}, u32[]{:S(2)}) collective-permute-start(f32[2,1,8,128]{3,1,2,0:T(1,128)S(1)} %pad_maximum_fusion.14), channel_id=1, source_target_pairs={{0,8},{8,16},{16,24},{24,32},{32,40},{40,48},{48,56},{56,64},{64,7... | collective-permute-start | bytes 24584 | tf_op jit(solution)/shard_map/ppermute | solution.py:30
  13.2 1.0 constant_dynamic-slice_fusion.1
  14.2 3.4 %collective-permute-start.10 = (f32[3,4,8,1]{3,2,1,0:T(8,128)S(1)}, f32[3,4,8,1]{3,2,1,0:T(8,128)S(1)}, u32[]{:S(2)}, u32[]{:S(2)}) collective-permute-start(f32[3,4,8,1]{3,2,1,0:T(8,128)S(1)} %get-tuple-element.92), channel_id=1, source_target_pairs={{0,128},{128,256},{256,384},{1,129},{129,257},{257,385},{2,130},{1... | collective-permute-start | bytes 1160 | tf_op jit(solution)/shard_map/ppermute | solution.py:18
  17.6 1.3 collective-permute-start.11
  18.9 1.0 copy.414
  20.0 3.5 %collective-permute-start.2 = (f32[12,1,8,128]{3,1,2,0:T(1,128)S(1)}, f32[12,1,8,128]{3,1,2,0:T(1,128)S(1)}, u32[]{:S(2)}, u32[]{:S(2)}) collective-permute-start(f32[12,1,8,128]{3,1,2,0:T(1,128)S(1)} %get-tuple-element.66), channel_id=1, source_target_pairs={{0,8},{8,16},{16,24},{24,32},{32,40},{40,48},{48,56},{56,64},{64,7... | collective-permute-start | bytes 147464 | tf_op jit(solution)/shard_map/ppermute | solution.py:18
  24.2 0.9 constant_dynamic-slice_fusion.2
  25.8 0.7 fusion.74
  26.7 0.7 iota_compare_fusion.5
  27.4 0.7 broadcast_multiply_fusion.1
  28.4 0.8 select_reduce_fusion
  29.2 0.8 dynamic-slice_multiply_fusion
  30.8 4.7 %collective-permute-start.12 = (f32[3,1,8,34]{3,2,1,0:T(8,128)S(1)}, f32[3,1,8,34]{3,2,1,0:T(8,128)S(1)}, u32[]{:S(2)}, u32[]{:S(2)}) collective-permute-start(f32[3,1,8,34]{3,2,1,0:T(8,128)S(1)} %get-tuple-element.70), channel_id=1, source_target_pairs={{0,8},{8,16},{16,24},{24,32},{32,40},{40,48},{48,56},{56,64},{64,7... | collective-permute-start | bytes 9800 | tf_op jit(solution)/shard_map/ppermute | solution.py:18
  35.5 1.9 collective-permute-start.13
  37.4 3.6 %collective-permute-done.13 = f32[3,1,8,34]{3,2,1,0:T(8,128)S(1)} collective-permute-done((f32[3,1,8,34]{3,2,1,0:T(8,128)S(1)}, f32[3,1,8,34]{3,2,1,0:T(8,128)S(1)}, u32[]{:S(2)}, u32[]{:S(2)}) %collective-permute-start.13) | collective-permute-done | bytes 3296 | tf_op jit(solution)/shard_map/ppermute | solution.py:20
  41.2 2.4 %collective-permute-start.14 = (f32[3,6,1,34]{3,1,2,0:T(8,128)S(1)}, f32[3,6,1,34]{3,1,2,0:T(8,128)S(1)}, u32[]{:S(2)}, u32[]{:S(2)}) collective-permute-start(f32[3,6,1,34]{3,1,2,0:T(8,128)S(1)} %get-tuple-element.80), channel_id=1, source_target_pairs={{0,1},{1,2},{2,3},{3,4},{4,5},{5,6},{6,7},{8,9},{9,10},{10,11},{11... | collective-permute-start | bytes 7352 | tf_op jit(solution)/shard_map/ppermute | solution.py:18
  43.7 1.3 collective-permute-start.15
  45.1 2.2 %collective-permute-start.3 = (f32[12,1,8,128]{3,1,2,0:T(1,128)S(1)}, f32[12,1,8,128]{3,1,2,0:T(1,128)S(1)}, u32[]{:S(2)}, u32[]{:S(2)}) collective-permute-start(f32[12,1,8,128]{3,1,2,0:T(1,128)S(1)} %get-tuple-element.67), channel_id=1, source_target_pairs={{8,0},{16,8},{24,16},{32,24},{40,32},{48,40},{56,48},{64,56},{72,6... | collective-permute-start | bytes 147464 | tf_op jit(solution)/shard_map/ppermute | solution.py:20
  47.3 1.2 collective-permute-done.15
  49.6 4.6 %collective-permute-start.16 = (f32[3,4,8,1]{3,2,1,0:T(8,128)S(1)}, f32[3,4,8,1]{3,2,1,0:T(8,128)S(1)}, u32[]{:S(2)}, u32[]{:S(2)}) collective-permute-start(f32[3,4,8,1]{3,2,1,0:T(8,128)S(1)} %get-tuple-element.90), channel_id=1, source_target_pairs={{0,128},{128,256},{256,384},{1,129},{129,257},{257,385},{2,130},{1... | collective-permute-start | bytes 1160 | tf_op jit(solution)/shard_map/ppermute | solution.py:18
  54.1 1.3 collective-permute-start.17
  55.9 4.3 %collective-permute-done.17 = f32[3,4,8,1]{3,2,1,0:T(8,128)S(1)} collective-permute-done((f32[3,4,8,1]{3,2,1,0:T(8,128)S(1)}, f32[3,4,8,1]{3,2,1,0:T(8,128)S(1)}, u32[]{:S(2)}, u32[]{:S(2)}) %collective-permute-start.17) | collective-permute-done | bytes 416 | tf_op jit(solution)/shard_map/ppermute | solution.py:20
  60.2 2.6 %collective-permute-start.18 = (f32[3,1,8,34]{3,2,1,0:T(8,128)S(1)}, f32[3,1,8,34]{3,2,1,0:T(8,128)S(1)}, u32[]{:S(2)}, u32[]{:S(2)}) collective-permute-start(f32[3,1,8,34]{3,2,1,0:T(8,128)S(1)} %get-tuple-element.68), channel_id=1, source_target_pairs={{0,8},{8,16},{16,24},{24,32},{32,40},{40,48},{48,56},{56,64},{64,7... | collective-permute-start | bytes 9800 | tf_op jit(solution)/shard_map/ppermute | solution.py:18
  62.8 3.3 %collective-permute-start.19 = (f32[3,1,8,34]{3,2,1,0:T(8,128)S(1)}, f32[3,1,8,34]{3,2,1,0:T(8,128)S(1)}, u32[]{:S(2)}, u32[]{:S(2)}) collective-permute-start(f32[3,1,8,34]{3,2,1,0:T(8,128)S(1)} %get-tuple-element.69), channel_id=1, source_target_pairs={{8,0},{16,8},{24,16},{32,24},{40,32},{48,40},{56,48},{64,56},{72,6... | collective-permute-start | bytes 9800 | tf_op jit(solution)/shard_map/ppermute | solution.py:20
  66.1 17.6 %all-gather = f32[1,6,4,8,128]{3,2,1,0,4:T(4,128)S(1)} all-gather(f32[1,6,4,8,32]{3,2,1,0,4:T(4,128)S(1)} %copy.434), channel_id=2, replica_groups=mesh['grp'=4,'gx'=16,'gy'=8] {'grp'}, dimensions={4}, use_global_device_ids=true | all-gather | bytes 122880 | tf_op jit(solution)/shard_map/all_gather | solution.py:179
  84.4 1.5 collective-permute-start.20
  85.9 1.3 collective-permute-start.21
  87.3 5.0 %collective-permute-done.21 = f32[3,6,1,34]{3,1,2,0:T(8,128)S(1)} collective-permute-done((f32[3,6,1,34]{3,1,2,0:T(8,128)S(1)}, f32[3,6,1,34]{3,1,2,0:T(8,128)S(1)}, u32[]{:S(2)}, u32[]{:S(2)}) %collective-permute-start.21) | collective-permute-done | bytes 2480 | tf_op jit(solution)/shard_map/ppermute | solution.py:20
  92.9 4.3 %collective-permute-start.4 = (f32[12,6,1,128]{3,1,2,0:T(8,128)S(1)}, f32[12,6,1,128]{3,1,2,0:T(8,128)S(1)}, u32[]{:S(2)}, u32[]{:S(2)}) collective-permute-start(f32[12,6,1,128]{3,1,2,0:T(8,128)S(1)} %get-tuple-element.59), channel_id=1, source_target_pairs={{0,1},{1,2},{2,3},{3,4},{4,5},{5,6},{6,7},{8,9},{9,10},{10,11},{11... | collective-permute-start | bytes 110600 | tf_op jit(solution)/shard_map/ppermute | solution.py:18
  97.3 1.3 collective-permute-start.5
  98.6 18.0 %all-gather.1 = f32[1,6,4,8,128]{3,2,1,0,4:T(4,128)S(1)} all-gather(f32[1,6,4,8,32]{3,2,1,0,4:T(4,128)S(1)} %copy.451), channel_id=3, replica_groups=mesh['grp'=4,'gx'=16,'gy'=8] {'grp'}, dimensions={4}, use_global_device_ids=true | all-gather | bytes 122880 | tf_op jit(solution)/shard_map/all_gather | solution.py:179
  116.6 1.2 copy.452
  117.9 0.7 select_maximum_fusion.4
  120.7 3.5 %collective-permute-start.6 = (f32[12,1,8,128]{3,2,1,0:T(8,128)S(1)}, f32[12,1,8,128]{3,2,1,0:T(8,128)S(1)}, u32[]{:S(2)}, u32[]{:S(2)}) collective-permute-start(f32[12,1,8,128]{3,2,1,0:T(8,128)S(1)} %get-tuple-element.64), channel_id=1, source_target_pairs={{0,8},{8,16},{16,24},{24,32},{32,40},{40,48},{48,56},{56,64},{64,7... | collective-permute-start | bytes 147464 | tf_op jit(solution)/shard_map/ppermute | solution.py:18
  124.2 2.4 %collective-permute-start.7 = (f32[12,1,8,128]{3,2,1,0:T(8,128)S(1)}, f32[12,1,8,128]{3,2,1,0:T(8,128)S(1)}, u32[]{:S(2)}, u32[]{:S(2)}) collective-permute-start(f32[12,1,8,128]{3,2,1,0:T(8,128)S(1)} %get-tuple-element.65), channel_id=1, source_target_pairs={{8,0},{16,8},{24,16},{32,24},{40,32},{48,40},{56,48},{64,56},{72,6... | collective-permute-start | bytes 147464 | tf_op jit(solution)/shard_map/ppermute | solution.py:20
  127.2 4.8 %collective-permute-done.7 = f32[12,1,8,128]{3,2,1,0:T(8,128)S(1)} collective-permute-done((f32[12,1,8,128]{3,2,1,0:T(8,128)S(1)}, f32[12,1,8,128]{3,2,1,0:T(8,128)S(1)}, u32[]{:S(2)}, u32[]{:S(2)}) %collective-permute-start.7) | collective-permute-done | bytes 49184 | tf_op jit(solution)/shard_map/ppermute | solution.py:20
  132.0 1.3 collective-permute-start.8
  133.3 1.5 collective-permute-start.9
  134.8 3.6 %collective-permute-done.9 = f32[12,6,1,128]{3,2,1,0:T(1,128)S(1)} collective-permute-done((f32[12,6,1,128]{3,2,1,0:T(1,128)S(1)}, f32[12,6,1,128]{3,2,1,0:T(1,128)S(1)}, u32[]{:S(2)}, u32[]{:S(2)}) %collective-permute-start.9) | collective-permute-done | bytes 36896 | tf_op jit(solution)/shard_map/ppermute | solution.py:20
  138.4 0.7 select_maximum_fusion
  139.7 2.0 %copy_subtract_fusion.1 = (f32[4,3,5,9,129]{4,2,3,0,1:T(8,128)S(1)}, f32[4,3,5,9,129]{4,2,3,0,1:T(8,128)S(1)}, f32[4,3,5,9,129]{4,2,3,0,1:T(8,128)S(1)}) fusion(f32[4,3,5,9,129]{4,3,2,1,0:T(8,128)S(1)} %get-tuple-element.34, f32[4,3,5,9,129]{4,3,2,1,0:T(8,128)S(1)} %get-tuple-element.35, f32[4,3,5,9,129]{4,3,2,1,0:T(8,128)S(1)} %get-tuple-element.37, ...), kind=kLoop, calls=%fused_computation.16 | loop fusion | flops 208980 | bytes 1950480 | tf_op jit(solution)/shard_map/sub | solution.py:50
  143.4 1.0 reshape.361
  145.1 0.7 copy.463
  145.8 46.9 %reduce-scatter.4.cloned.1.call-done = f32[32,64]{1,0:T(8,128)} async-done(((f32[128,64]{1,0:T(8,128)}), f32[32,64]{1,0:T(8,128)}) %reduce-scatter.4.cloned.1.call-update) | async-done | bytes 8208
  192.6 0.8 reshape.362
  193.5 0.7 copy.465
  (132 shorter events, 9.9 us)
Async XLA Ops:
  7.2 37.8 %copy-start.7 = (f32[256,3]{0,1:T(4,128)S(1)}, f32[256,3]{0,1:T(4,128)}, u32[]{:S(2)}) copy-start(f32[256,3]{0,1:T(4,128)} %param.24) | copy-start | bytes 9220
  7.2 185.5 %reduce-scatter.4.cloned.1.call-start = ((), (), s32[]{:S(2)}) async-start(), calls=%async_computation.1 | async-start | bytes 81920
  8.0 40.8 %collective-permute-start = (f32[2,4,1,128]{3,1,2,0:T(4,128)S(1)}, f32[2,4,1,128]{3,1,2,0:T(4,128)S(1)}, u32[]{:S(2)}, u32[]{:S(2)}) collective-permute-start(f32[2,4,1,128]{3,1,2,0:T(4,128)S(1)} %pad_maximum_fusion.15), channel_id=1, source_target_pairs={{0,1},{1,2},{2,3},{3,4},{4,5},{5,6},{6,7},{8,9},{9,10},{10,11},{11... | collective-permute-start | bytes 12296 | tf_op jit(solution)/shard_map/ppermute | solution.py:30
  9.7 39.0 %collective-permute-start.1 = (f32[2,1,8,128]{3,1,2,0:T(1,128)S(1)}, f32[2,1,8,128]{3,1,2,0:T(1,128)S(1)}, u32[]{:S(2)}, u32[]{:S(2)}) collective-permute-start(f32[2,1,8,128]{3,1,2,0:T(1,128)S(1)} %pad_maximum_fusion.14), channel_id=1, source_target_pairs={{0,8},{8,16},{16,24},{24,32},{32,40},{40,48},{48,56},{56,64},{64,7... | collective-permute-start | bytes 24584 | tf_op jit(solution)/shard_map/ppermute | solution.py:30
  14.2 16.5 %collective-permute-start.10 = (f32[3,4,8,1]{3,2,1,0:T(8,128)S(1)}, f32[3,4,8,1]{3,2,1,0:T(8,128)S(1)}, u32[]{:S(2)}, u32[]{:S(2)}) collective-permute-start(f32[3,4,8,1]{3,2,1,0:T(8,128)S(1)} %get-tuple-element.92), channel_id=1, source_target_pairs={{0,128},{128,256},{256,384},{1,129},{129,257},{257,385},{2,130},{1... | collective-permute-start | bytes 1160 | tf_op jit(solution)/shard_map/ppermute | solution.py:18
  17.6 13.1 %collective-permute-start.11 = (f32[3,4,8,1]{3,2,1,0:T(8,128)S(1)}, f32[3,4,8,1]{3,2,1,0:T(8,128)S(1)}, u32[]{:S(2)}, u32[]{:S(2)}) collective-permute-start(f32[3,4,8,1]{3,2,1,0:T(8,128)S(1)} %get-tuple-element.93), channel_id=1, source_target_pairs={{128,0},{256,128},{384,256},{129,1},{257,129},{385,257},{130,2},{2... | collective-permute-start | bytes 1160 | tf_op jit(solution)/shard_map/ppermute | solution.py:20
  20.0 72.9 %collective-permute-start.2 = (f32[12,1,8,128]{3,1,2,0:T(1,128)S(1)}, f32[12,1,8,128]{3,1,2,0:T(1,128)S(1)}, u32[]{:S(2)}, u32[]{:S(2)}) collective-permute-start(f32[12,1,8,128]{3,1,2,0:T(1,128)S(1)} %get-tuple-element.66), channel_id=1, source_target_pairs={{0,8},{8,16},{16,24},{24,32},{32,40},{40,48},{48,56},{56,64},{64,7... | collective-permute-start | bytes 147464 | tf_op jit(solution)/shard_map/ppermute | solution.py:18
  30.8 6.6 %collective-permute-start.12 = (f32[3,1,8,34]{3,2,1,0:T(8,128)S(1)}, f32[3,1,8,34]{3,2,1,0:T(8,128)S(1)}, u32[]{:S(2)}, u32[]{:S(2)}) collective-permute-start(f32[3,1,8,34]{3,2,1,0:T(8,128)S(1)} %get-tuple-element.70), channel_id=1, source_target_pairs={{0,8},{8,16},{16,24},{24,32},{32,40},{40,48},{48,56},{56,64},{64,7... | collective-permute-start | bytes 9800 | tf_op jit(solution)/shard_map/ppermute | solution.py:18
  35.5 5.6 %collective-permute-start.13 = (f32[3,1,8,34]{3,2,1,0:T(8,128)S(1)}, f32[3,1,8,34]{3,2,1,0:T(8,128)S(1)}, u32[]{:S(2)}, u32[]{:S(2)}) collective-permute-start(f32[3,1,8,34]{3,2,1,0:T(8,128)S(1)} %get-tuple-element.71), channel_id=1, source_target_pairs={{8,0},{16,8},{24,16},{32,24},{40,32},{48,40},{56,48},{64,56},{72,6... | collective-permute-start | bytes 9800 | tf_op jit(solution)/shard_map/ppermute | solution.py:20
  41.2 8.2 %copy-start.1 = (f32[3,4,8,128]{3,2,1,0:T(8,128)S(1)}, f32[3,4,8,128]{3,2,1,0:T(8,128)}, u32[]{:S(2)}) copy-start(f32[3,4,8,128]{3,2,1,0:T(8,128)} %param.15) | copy-start | bytes 147460
  41.2 8.2 %copy-start.6 = (f32[3,4,8,128]{3,2,1,0:T(8,128)S(1)}, f32[3,4,8,128]{3,2,1,0:T(8,128)}, u32[]{:S(2)}) copy-start(f32[3,4,8,128]{3,2,1,0:T(8,128)} %param.16) | copy-start | bytes 147460
  41.2 3.9 %collective-permute-start.14 = (f32[3,6,1,34]{3,1,2,0:T(8,128)S(1)}, f32[3,6,1,34]{3,1,2,0:T(8,128)S(1)}, u32[]{:S(2)}, u32[]{:S(2)}) collective-permute-start(f32[3,6,1,34]{3,1,2,0:T(8,128)S(1)} %get-tuple-element.80), channel_id=1, source_target_pairs={{0,1},{1,2},{2,3},{3,4},{4,5},{5,6},{6,7},{8,9},{9,10},{10,11},{11... | collective-permute-start | bytes 7352 | tf_op jit(solution)/shard_map/ppermute | solution.py:18
  43.7 4.9 %collective-permute-start.15 = (f32[3,6,1,34]{3,1,2,0:T(8,128)S(1)}, f32[3,6,1,34]{3,1,2,0:T(8,128)S(1)}, u32[]{:S(2)}, u32[]{:S(2)}) collective-permute-start(f32[3,6,1,34]{3,1,2,0:T(8,128)S(1)} %get-tuple-element.81), channel_id=1, source_target_pairs={{1,0},{2,1},{3,2},{4,3},{5,4},{6,5},{7,6},{9,8},{10,9},{11,10},{12... | collective-permute-start | bytes 7352 | tf_op jit(solution)/shard_map/ppermute | solution.py:20
  45.1 47.8 %collective-permute-start.3 = (f32[12,1,8,128]{3,1,2,0:T(1,128)S(1)}, f32[12,1,8,128]{3,1,2,0:T(1,128)S(1)}, u32[]{:S(2)}, u32[]{:S(2)}) collective-permute-start(f32[12,1,8,128]{3,1,2,0:T(1,128)S(1)} %get-tuple-element.67), channel_id=1, source_target_pairs={{8,0},{16,8},{24,16},{32,24},{40,32},{48,40},{56,48},{64,56},{72,6... | collective-permute-start | bytes 147464 | tf_op jit(solution)/shard_map/ppermute | solution.py:20
  49.6 6.3 %collective-permute-start.16 = (f32[3,4,8,1]{3,2,1,0:T(8,128)S(1)}, f32[3,4,8,1]{3,2,1,0:T(8,128)S(1)}, u32[]{:S(2)}, u32[]{:S(2)}) collective-permute-start(f32[3,4,8,1]{3,2,1,0:T(8,128)S(1)} %get-tuple-element.90), channel_id=1, source_target_pairs={{0,128},{128,256},{256,384},{1,129},{129,257},{257,385},{2,130},{1... | collective-permute-start | bytes 1160 | tf_op jit(solution)/shard_map/ppermute | solution.py:18
  54.1 6.0 %collective-permute-start.17 = (f32[3,4,8,1]{3,2,1,0:T(8,128)S(1)}, f32[3,4,8,1]{3,2,1,0:T(8,128)S(1)}, u32[]{:S(2)}, u32[]{:S(2)}) collective-permute-start(f32[3,4,8,1]{3,2,1,0:T(8,128)S(1)} %get-tuple-element.91), channel_id=1, source_target_pairs={{128,0},{256,128},{384,256},{129,1},{257,129},{385,257},{130,2},{2... | collective-permute-start | bytes 1160 | tf_op jit(solution)/shard_map/ppermute | solution.py:20
  60.2 24.1 %collective-permute-start.18 = (f32[3,1,8,34]{3,2,1,0:T(8,128)S(1)}, f32[3,1,8,34]{3,2,1,0:T(8,128)S(1)}, u32[]{:S(2)}, u32[]{:S(2)}) collective-permute-start(f32[3,1,8,34]{3,2,1,0:T(8,128)S(1)} %get-tuple-element.68), channel_id=1, source_target_pairs={{0,8},{8,16},{16,24},{24,32},{32,40},{40,48},{48,56},{56,64},{64,7... | collective-permute-start | bytes 9800 | tf_op jit(solution)/shard_map/ppermute | solution.py:18
  62.8 21.5 %collective-permute-start.19 = (f32[3,1,8,34]{3,2,1,0:T(8,128)S(1)}, f32[3,1,8,34]{3,2,1,0:T(8,128)S(1)}, u32[]{:S(2)}, u32[]{:S(2)}) collective-permute-start(f32[3,1,8,34]{3,2,1,0:T(8,128)S(1)} %get-tuple-element.69), channel_id=1, source_target_pairs={{8,0},{16,8},{24,16},{32,24},{40,32},{48,40},{56,48},{64,56},{72,6... | collective-permute-start | bytes 9800 | tf_op jit(solution)/shard_map/ppermute | solution.py:20
  84.3 50.5 %copy-start.2 = (f32[1,6,4,8,128]{4,2,3,1,0:T(4,128)}, f32[1,6,4,8,128]{4,2,3,1,0:T(4,128)S(1)}, u32[]{:S(2)}) copy-start(f32[1,6,4,8,128]{4,2,3,1,0:T(4,128)S(1)} %copy.435) | copy-start | bytes 294916
  84.4 2.8 %collective-permute-start.20 = (f32[3,6,1,34]{3,1,2,0:T(8,128)S(1)}, f32[3,6,1,34]{3,1,2,0:T(8,128)S(1)}, u32[]{:S(2)}, u32[]{:S(2)}) collective-permute-start(f32[3,6,1,34]{3,1,2,0:T(8,128)S(1)} %get-tuple-element.78), channel_id=1, source_target_pairs={{0,1},{1,2},{2,3},{3,4},{4,5},{5,6},{6,7},{8,9},{9,10},{10,11},{11... | collective-permute-start | bytes 7352 | tf_op jit(solution)/shard_map/ppermute | solution.py:18
  85.9 6.4 %collective-permute-start.21 = (f32[3,6,1,34]{3,1,2,0:T(8,128)S(1)}, f32[3,6,1,34]{3,1,2,0:T(8,128)S(1)}, u32[]{:S(2)}, u32[]{:S(2)}) collective-permute-start(f32[3,6,1,34]{3,1,2,0:T(8,128)S(1)} %get-tuple-element.79), channel_id=1, source_target_pairs={{1,0},{2,1},{3,2},{4,3},{5,4},{6,5},{7,6},{9,8},{10,9},{11,10},{12... | collective-permute-start | bytes 7352 | tf_op jit(solution)/shard_map/ppermute | solution.py:20
  92.9 24.9 %collective-permute-start.4 = (f32[12,6,1,128]{3,1,2,0:T(8,128)S(1)}, f32[12,6,1,128]{3,1,2,0:T(8,128)S(1)}, u32[]{:S(2)}, u32[]{:S(2)}) collective-permute-start(f32[12,6,1,128]{3,1,2,0:T(8,128)S(1)} %get-tuple-element.59), channel_id=1, source_target_pairs={{0,1},{1,2},{2,3},{3,4},{4,5},{5,6},{6,7},{8,9},{9,10},{10,11},{11... | collective-permute-start | bytes 110600 | tf_op jit(solution)/shard_map/ppermute | solution.py:18
  97.3 20.6 %collective-permute-start.5 = (f32[12,6,1,128]{3,1,2,0:T(8,128)S(1)}, f32[12,6,1,128]{3,1,2,0:T(8,128)S(1)}, u32[]{:S(2)}, u32[]{:S(2)}) collective-permute-start(f32[12,6,1,128]{3,1,2,0:T(8,128)S(1)} %get-tuple-element.60), channel_id=1, source_target_pairs={{1,0},{2,1},{3,2},{4,3},{5,4},{6,5},{7,6},{9,8},{10,9},{11,10},{12... | collective-permute-start | bytes 110600 | tf_op jit(solution)/shard_map/ppermute | solution.py:20
  119.5 0.9 copy-start
  119.5 1.0 copy-start.5
  120.7 6.5 %collective-permute-start.6 = (f32[12,1,8,128]{3,2,1,0:T(8,128)S(1)}, f32[12,1,8,128]{3,2,1,0:T(8,128)S(1)}, u32[]{:S(2)}, u32[]{:S(2)}) collective-permute-start(f32[12,1,8,128]{3,2,1,0:T(8,128)S(1)} %get-tuple-element.64), channel_id=1, source_target_pairs={{0,8},{8,16},{16,24},{24,32},{32,40},{40,48},{48,56},{56,64},{64,7... | collective-permute-start | bytes 147464 | tf_op jit(solution)/shard_map/ppermute | solution.py:18
  124.2 7.8 %collective-permute-start.7 = (f32[12,1,8,128]{3,2,1,0:T(8,128)S(1)}, f32[12,1,8,128]{3,2,1,0:T(8,128)S(1)}, u32[]{:S(2)}, u32[]{:S(2)}) collective-permute-start(f32[12,1,8,128]{3,2,1,0:T(8,128)S(1)} %get-tuple-element.65), channel_id=1, source_target_pairs={{8,0},{16,8},{24,16},{32,24},{40,32},{48,40},{56,48},{64,56},{72,6... | collective-permute-start | bytes 147464 | tf_op jit(solution)/shard_map/ppermute | solution.py:20
  132.0 2.8 %collective-permute-start.8 = (f32[12,6,1,128]{3,2,1,0:T(1,128)S(1)}, f32[12,6,1,128]{3,2,1,0:T(1,128)S(1)}, u32[]{:S(2)}, u32[]{:S(2)}) collective-permute-start(f32[12,6,1,128]{3,2,1,0:T(1,128)S(1)} %get-tuple-element.54), channel_id=1, source_target_pairs={{0,1},{1,2},{2,3},{3,4},{4,5},{5,6},{6,7},{8,9},{9,10},{10,11},{11... | collective-permute-start | bytes 110600 | tf_op jit(solution)/shard_map/ppermute | solution.py:18
  133.3 5.1 %collective-permute-start.9 = (f32[12,6,1,128]{3,2,1,0:T(1,128)S(1)}, f32[12,6,1,128]{3,2,1,0:T(1,128)S(1)}, u32[]{:S(2)}, u32[]{:S(2)}) collective-permute-start(f32[12,6,1,128]{3,2,1,0:T(1,128)S(1)} %get-tuple-element.55), channel_id=1, source_target_pairs={{1,0},{2,1},{3,2},{4,3},{5,4},{6,5},{7,6},{9,8},{10,9},{11,10},{12... | collective-permute-start | bytes 110600 | tf_op jit(solution)/shard_map/ppermute | solution.py:20
  142.0 0.9 copy-start.4
  142.1 0.9 copy-start.3
  142.1 0.9 copy-start.8
Sparse Core Ops, SparseCore 0:
  144.6 48.0 reduce-scatter.3
where the time goes:
time: 202 us; the launch traced here: 201 us
  waiting for transfers between devices  69.5 us (34%)
  starting transfers between devices  54.6 us (27%)
  blocking collectives  35.6 us (18%)
  between operations  16.4 us (8%)
  other arithmetic  13.2 us (7%)
  local copies, waits for them, and re-layouts  11.7 us (6%)
    unnamed x2, waiting for transfers between devices  46.9 us
    all_gather x2, blocking collectives, local(): master_whole = lax.all_gather(master_strain[0], 'grp', axis=3, tiled=True)  35.6 us
    ppermute x10, starting transfers between devices, with_halo(): lax.ppermute(tail, axis, [(i, (i + 1) % count) for i in range(ends)])  31.7 us
    ppermute x10, waiting for transfers between devices, with_halo(): lax.ppermute(head, axis, [((i + 1) % count, i) for i in range(ends)])  22.5 us
    ppermute x10, starting transfers between devices, with_halo(): lax.ppermute(head, axis, [((i + 1) % count, i) for i in range(ends)])  17.7 us
    unnamed x36, local copies, waits for them, and re-layouts  5.5 us
    ppermute x2, starting transfers between devices, passed_along(): return lax.ppermute(value, axis, pairs)  5.22 us
  transfers between devices with their start and end apart: 23, of which 8 were waited for; matrix products, arithmetic and copies ran while one was open for 7% of the time, Pallas kernels for 0%

commit v1 on v0

--- a/solution.py
+++ b/solution.py
@@ -1,3 +1,4 @@
+import functools
 import jax
 import jax.numpy as jnp
 from jax import lax
@@ -5,6 +6,16 @@
 
 STEPS = 2
 time_step_sq = 0.0625
+
+
+def fix_face_all(message, dim_at):
+    reply = jax.lax.psum(1, "grp")
+    wide_out = jnp.stack([message] * reply, axis=0)
+    v1 = jax.lax.all_to_all(wide_out, "grp", 0, 0)
+    return jnp.concatenate(v1, axis=dim_at)
+
+
+_make_lines = functools.partial(fix_face_all, dim_at=3)
 
 
 def with_halo(cells, sides, width):
@@ -176,7 +187,7 @@
     for instant in range(STEPS):
         grown = with_halo(master_now, (("grp", 3), ("gx", 1), ("gy", 2)), 1)
         master_force, master_strain = stencil(grown[None], lame_share, shear_share)
-        master_whole = lax.all_gather(master_strain[0], "grp", axis=3, tiled=True)
+        master_whole = _make_lines(master_strain[0])
         if instant + 1 < STEPS:
             master_next = advance(
                 master_now[None],

time: 202 us -> 181 us (0.90)
  blocking collectives: 35.6 us -> 0 us
  starting transfers between devices: 54.6 us -> 64.5 us
  other arithmetic: 13.2 us -> 17.6 us
    all_gather x2 -> x0, blocking collectives: 35.6 us -> none  [local(): master_whole = lax.all_gather(master_strain[0], 'grp', axis=3, tiled=True)]
    all_to_all x0 -> x2, starting transfers between devices: none -> 8.81 us  [fix_face_all(): v1 = jax.lax.all_to_all(wide_out, 'grp', 0, 0)]
    ppermute x10, waiting for transfers between devices: 22.5 us -> 20.2 us  [with_halo(): lax.ppermute(head, axis, [((i + 1) % count, i) for i in range(ends)])]
    unnamed x36 -> x31, local copies, waits for them, and re-layouts: 5.5 us -> 7.11 us
  transfers between devices with their start and end apart: 23 -> 25, of which waited for: 8 -> 8; matrix products, arithmetic and copies ran while one was open for 7% -> 11% of each run, Pallas kernels for 0% -> 0%
where the time goes in v1:
time: 181 us; the launch traced here: 180 us
  waiting for transfers between devices  69.5 us (38%)
  starting transfers between devices  64.5 us (36%)
  other arithmetic  17.6 us (10%)
  between operations  16.4 us (9%)
  local copies, waits for them, and re-layouts  11.7 us (6%)
    unnamed x2, waiting for transfers between devices  48.9 us
    ppermute x10, starting transfers between devices, with_halo(): lax.ppermute(tail, axis, [(i, (i + 1) % count) for i in range(ends)])  33.1 us
    ppermute x10, waiting for transfers between devices, with_halo(): lax.ppermute(head, axis, [((i + 1) % count, i) for i in range(ends)])  20.2 us
    ppermute x10, starting transfers between devices, with_halo(): lax.ppermute(head, axis, [((i + 1) % count, i) for i in range(ends)])  17.3 us
    all_to_all x2, starting transfers between devices, fix_face_all(): v1 = jax.lax.all_to_all(wide_out, 'grp', 0, 0)  8.81 us
    unnamed x31, local copies, waits for them, and re-layouts  7.11 us
    ppermute x2, starting transfers between devices, passed_along(): return lax.ppermute(value, axis, pairs)  5.22 us
  transfers between devices with their start and end apart: 25, of which 8 were waited for; matrix products, arithmetic and copies ran while one was open for 11% of the time, Pallas kernels for 0%

profile of v1, /device:TPU:8, one launch (start us, length us, event | category | flops | bytes accessed | tf_op | source)
XLA Modules:
  0.0 179.7 jit_solution(2158712157905923073)
XLA Ops:
  7.2 0.7 copy_bitcast_fusion
  7.9 1.7 collective-permute-start
  9.7 3.5 %collective-permute-start.1 = (f32[2,1,8,128]{3,1,2,0:T(1,128)S(1)}, f32[2,1,8,128]{3,1,2,0:T(1,128)S(1)}, u32[]{:S(2)}, u32[]{:S(2)}) collective-permute-start(f32[2,1,8,128]{3,1,2,0:T(1,128)S(1)} %pad_maximum_fusion.22), channel_id=1, source_target_pairs={{0,8},{8,16},{16,24},{24,32},{32,40},{40,48},{48,56},{56,64},{64,7... | collective-permute-start | bytes 24584 | tf_op jit(solution)/shard_map/ppermute | solution.py:41
  13.2 0.9 constant_dynamic-slice_fusion
  14.2 3.4 %collective-permute-start.10 = (f32[3,4,8,1]{3,1,2,0:T(4,128)S(1)}, f32[3,4,8,1]{3,1,2,0:T(4,128)S(1)}, u32[]{:S(2)}, u32[]{:S(2)}) collective-permute-start(f32[3,4,8,1]{3,1,2,0:T(4,128)S(1)} %get-tuple-element.88), channel_id=1, source_target_pairs={{0,128},{128,256},{256,384},{1,129},{129,257},{257,385},{2,130},{1... | collective-permute-start | bytes 1160 | tf_op jit(solution)/shard_map/ppermute | solution.py:29
  17.6 1.3 collective-permute-start.11
  18.9 1.0 copy.221
  20.0 3.5 %collective-permute-start.2 = (f32[12,1,8,128]{3,1,2,0:T(1,128)S(1)}, f32[12,1,8,128]{3,1,2,0:T(1,128)S(1)}, u32[]{:S(2)}, u32[]{:S(2)}) collective-permute-start(f32[12,1,8,128]{3,1,2,0:T(1,128)S(1)} %get-tuple-element.62), channel_id=1, source_target_pairs={{0,8},{8,16},{16,24},{24,32},{32,40},{40,48},{48,56},{56,64},{64,7... | collective-permute-start | bytes 147464 | tf_op jit(solution)/shard_map/ppermute | solution.py:29
  25.8 0.7 iota_compare_fusion.5
  27.6 0.8 select_reduce_fusion
  28.4 0.8 dynamic-slice_multiply_fusion
  30.0 4.7 %collective-permute-start.12 = (f32[3,1,8,34]{3,1,2,0:T(1,128)S(1)}, f32[3,1,8,34]{3,1,2,0:T(1,128)S(1)}, u32[]{:S(2)}, u32[]{:S(2)}) collective-permute-start(f32[3,1,8,34]{3,1,2,0:T(1,128)S(1)} %get-tuple-element.70), channel_id=1, source_target_pairs={{0,8},{8,16},{16,24},{24,32},{32,40},{40,48},{48,56},{56,64},{64,7... | collective-permute-start | bytes 9800 | tf_op jit(solution)/shard_map/ppermute | solution.py:29
  34.8 1.9 %collective-permute-start.13 = (f32[3,1,8,34]{3,1,2,0:T(1,128)S(1)}, f32[3,1,8,34]{3,1,2,0:T(1,128)S(1)}, u32[]{:S(2)}, u32[]{:S(2)}) collective-permute-start(f32[3,1,8,34]{3,1,2,0:T(1,128)S(1)} %get-tuple-element.71), channel_id=1, source_target_pairs={{8,0},{16,8},{24,16},{32,24},{40,32},{48,40},{56,48},{64,56},{72,6... | collective-permute-start | bytes 9800 | tf_op jit(solution)/shard_map/ppermute | solution.py:31
  36.7 3.6 %collective-permute-done.13 = f32[3,1,8,34]{3,1,2,0:T(1,128)S(1)} collective-permute-done((f32[3,1,8,34]{3,1,2,0:T(1,128)S(1)}, f32[3,1,8,34]{3,1,2,0:T(1,128)S(1)}, u32[]{:S(2)}, u32[]{:S(2)}) %collective-permute-start.13) | collective-permute-done | bytes 3296 | tf_op jit(solution)/shard_map/ppermute | solution.py:31
  40.4 2.3 %collective-permute-start.14 = (f32[3,6,1,34]{3,1,2,0:T(8,128)S(1)}, f32[3,6,1,34]{3,1,2,0:T(8,128)S(1)}, u32[]{:S(2)}, u32[]{:S(2)}) collective-permute-start(f32[3,6,1,34]{3,1,2,0:T(8,128)S(1)} %get-tuple-element.66), channel_id=1, source_target_pairs={{0,1},{1,2},{2,3},{3,4},{4,5},{5,6},{6,7},{8,9},{9,10},{10,11},{11... | collective-permute-start | bytes 7352 | tf_op jit(solution)/shard_map/ppermute | solution.py:29
  42.7 1.3 collective-permute-start.15
  44.2 2.2 %collective-permute-start.3 = (f32[12,1,8,128]{3,1,2,0:T(1,128)S(1)}, f32[12,1,8,128]{3,1,2,0:T(1,128)S(1)}, u32[]{:S(2)}, u32[]{:S(2)}) collective-permute-start(f32[12,1,8,128]{3,1,2,0:T(1,128)S(1)} %get-tuple-element.63), channel_id=1, source_target_pairs={{8,0},{16,8},{24,16},{32,24},{40,32},{48,40},{56,48},{64,56},{72,6... | collective-permute-start | bytes 147464 | tf_op jit(solution)/shard_map/ppermute | solution.py:31
  46.4 1.2 collective-permute-done.15
  48.7 4.6 %collective-permute-start.16 = (f32[3,4,8,1]{3,1,2,0:T(4,128)S(1)}, f32[3,4,8,1]{3,1,2,0:T(4,128)S(1)}, u32[]{:S(2)}, u32[]{:S(2)}) collective-permute-start(f32[3,4,8,1]{3,1,2,0:T(4,128)S(1)} %get-tuple-element.86), channel_id=1, source_target_pairs={{0,128},{128,256},{256,384},{1,129},{129,257},{257,385},{2,130},{1... | collective-permute-start | bytes 1160 | tf_op jit(solution)/shard_map/ppermute | solution.py:29
  53.2 1.3 collective-permute-start.17
  55.0 4.3 %collective-permute-done.17 = f32[3,4,8,1]{3,1,2,0:T(4,128)S(1)} collective-permute-done((f32[3,4,8,1]{3,1,2,0:T(4,128)S(1)}, f32[3,4,8,1]{3,1,2,0:T(4,128)S(1)}, u32[]{:S(2)}, u32[]{:S(2)}) %collective-permute-start.17) | collective-permute-done | bytes 416 | tf_op jit(solution)/shard_map/ppermute | solution.py:31
  59.4 2.6 %collective-permute-start.18 = (f32[3,1,8,34]{3,1,2,0:T(1,128)S(1)}, f32[3,1,8,34]{3,1,2,0:T(1,128)S(1)}, u32[]{:S(2)}, u32[]{:S(2)}) collective-permute-start(f32[3,1,8,34]{3,1,2,0:T(1,128)S(1)} %get-tuple-element.68), channel_id=1, source_target_pairs={{0,8},{8,16},{16,24},{24,32},{32,40},{40,48},{48,56},{56,64},{64,7... | collective-permute-start | bytes 9800 | tf_op jit(solution)/shard_map/ppermute | solution.py:29
  62.0 3.3 %collective-permute-start.19 = (f32[3,1,8,34]{3,1,2,0:T(1,128)S(1)}, f32[3,1,8,34]{3,1,2,0:T(1,128)S(1)}, u32[]{:S(2)}, u32[]{:S(2)}) collective-permute-start(f32[3,1,8,34]{3,1,2,0:T(1,128)S(1)} %get-tuple-element.69), channel_id=1, source_target_pairs={{8,0},{16,8},{24,16},{32,24},{40,32},{48,40},{56,48},{64,56},{72,6... | collective-permute-start | bytes 9800 | tf_op jit(solution)/shard_map/ppermute | solution.py:31
  65.4 0.8 reshape.447
  66.3 4.0 %all-to-all-start = ((f32[4,1,6144]{2,1,0:T(1,128)}), f32[4,1,6144]{2,1,0:T(1,128)S(1)}, u32[]{:S(2)}, u32[]{:S(2)}) async-start(f32[4,1,6144]{2,1,0:T(1,128)} %reshape.447), calls=%async_computation | async-start | bytes 196608 | tf_op jit(solution)/shard_map/all_to_all | solution.py:14
  70.4 2.1 %collective-permute-start.20 = (f32[3,6,1,34]{3,1,2,0:T(8,128)S(1)}, f32[3,6,1,34]{3,1,2,0:T(8,128)S(1)}, u32[]{:S(2)}, u32[]{:S(2)}) collective-permute-start(f32[3,6,1,34]{3,1,2,0:T(8,128)S(1)} %get-tuple-element.64), channel_id=1, source_target_pairs={{0,1},{1,2},{2,3},{3,4},{4,5},{5,6},{6,7},{8,9},{9,10},{10,11},{11... | collective-permute-start | bytes 7352 | tf_op jit(solution)/shard_map/ppermute | solution.py:29
  72.5 1.3 collective-permute-start.21
  73.8 4.4 %collective-permute-done.21 = f32[3,6,1,34]{3,1,2,0:T(8,128)S(1)} collective-permute-done((f32[3,6,1,34]{3,1,2,0:T(8,128)S(1)}, f32[3,6,1,34]{3,1,2,0:T(8,128)S(1)}, u32[]{:S(2)}, u32[]{:S(2)}) %collective-permute-start.21) | collective-permute-done | bytes 2480 | tf_op jit(solution)/shard_map/ppermute | solution.py:31
  78.6 0.9 reshape.445
  79.5 4.3 %collective-permute-start.4 = (f32[12,6,1,128]{3,1,2,0:T(8,128)S(1)}, f32[12,6,1,128]{3,1,2,0:T(8,128)S(1)}, u32[]{:S(2)}, u32[]{:S(2)}) collective-permute-start(f32[12,6,1,128]{3,1,2,0:T(8,128)S(1)} %get-tuple-element.55), channel_id=1, source_target_pairs={{0,1},{1,2},{2,3},{3,4},{4,5},{5,6},{6,7},{8,9},{9,10},{10,11},{11... | collective-permute-start | bytes 110600 | tf_op jit(solution)/shard_map/ppermute | solution.py:29
  83.9 1.3 collective-permute-start.5
  85.2 4.8 %all-to-all-start.1 = ((f32[4,1,6144]{2,1,0:T(1,128)}), f32[4,1,6144]{2,1,0:T(1,128)S(1)}, u32[]{:S(2)}, u32[]{:S(2)}) async-start(f32[4,1,6144]{2,1,0:T(1,128)} %reshape.445), calls=%async_computation.1 | async-start | bytes 196608 | tf_op jit(solution)/shard_map/all_to_all | solution.py:14
  90.5 0.9 reduce.5
  91.8 0.7 select_maximum_fusion.4
  94.6 3.8 %collective-permute-start.6 = (f32[12,1,8,128]{3,2,1,0:T(8,128)S(1)}, f32[12,1,8,128]{3,2,1,0:T(8,128)S(1)}, u32[]{:S(2)}, u32[]{:S(2)}) collective-permute-start(f32[12,1,8,128]{3,2,1,0:T(8,128)S(1)} %get-tuple-element.60), channel_id=1, source_target_pairs={{0,8},{8,16},{16,24},{24,32},{32,40},{40,48},{48,56},{56,64},{64,7... | collective-permute-start | bytes 147464 | tf_op jit(solution)/shard_map/ppermute | solution.py:29
  98.5 2.0 %collective-permute-start.7 = (f32[12,1,8,128]{3,2,1,0:T(8,128)S(1)}, f32[12,1,8,128]{3,2,1,0:T(8,128)S(1)}, u32[]{:S(2)}, u32[]{:S(2)}) collective-permute-start(f32[12,1,8,128]{3,2,1,0:T(8,128)S(1)} %get-tuple-element.61), channel_id=1, source_target_pairs={{8,0},{16,8},{24,16},{32,24},{40,32},{48,40},{56,48},{64,56},{72,6... | collective-permute-start | bytes 147464 | tf_op jit(solution)/shard_map/ppermute | solution.py:31
  101.4 0.9 reduce.4
  102.4 3.8 %collective-permute-done.7 = f32[12,1,8,128]{3,2,1,0:T(8,128)S(1)} collective-permute-done((f32[12,1,8,128]{3,2,1,0:T(8,128)S(1)}, f32[12,1,8,128]{3,2,1,0:T(8,128)S(1)}, u32[]{:S(2)}, u32[]{:S(2)}) %collective-permute-start.7) | collective-permute-done | bytes 49184 | tf_op jit(solution)/shard_map/ppermute | solution.py:31
  106.3 1.9 %collective-permute-start.8 = (f32[12,6,1,128]{3,2,1,0:T(1,128)S(1)}, f32[12,6,1,128]{3,2,1,0:T(1,128)S(1)}, u32[]{:S(2)}, u32[]{:S(2)}) collective-permute-start(f32[12,6,1,128]{3,2,1,0:T(1,128)S(1)} %get-tuple-element.50), channel_id=1, source_target_pairs={{0,1},{1,2},{2,3},{3,4},{4,5},{5,6},{6,7},{8,9},{9,10},{10,11},{11... | collective-permute-start | bytes 110600 | tf_op jit(solution)/shard_map/ppermute | solution.py:29
  108.2 1.5 collective-permute-start.9
  109.9 2.9 %collective-permute-done.9 = f32[12,6,1,128]{3,2,1,0:T(1,128)S(1)} collective-permute-done((f32[12,6,1,128]{3,2,1,0:T(1,128)S(1)}, f32[12,6,1,128]{3,2,1,0:T(1,128)S(1)}, u32[]{:S(2)}, u32[]{:S(2)}) %collective-permute-start.9) | collective-permute-done | bytes 36896 | tf_op jit(solution)/shard_map/ppermute | solution.py:31
  114.0 2.0 %copy_subtract_fusion.1 = (f32[4,3,5,9,129]{4,2,3,0,1:T(8,128)S(1)}, f32[4,3,5,9,129]{4,2,3,0,1:T(8,128)S(1)}, f32[4,3,5,9,129]{4,2,3,0,1:T(8,128)S(1)}) fusion(f32[4,3,5,9,129]{4,3,2,1,0:T(8,128)S(1)} %get-tuple-element.30, f32[4,3,5,9,129]{4,3,2,1,0:T(8,128)S(1)} %get-tuple-element.31, f32[4,3,5,9,129]{4,3,2,1,0:T(8,128)S(1)} %get-tuple-element.33, ...), kind=kLoop, calls=%fused_computation.16 | loop fusion | flops 208980 | bytes 1950480 | tf_op jit(solution)/shard_map/sub | solution.py:61
  116.3 0.9 fusion.16
  119.0 1.0 reshape.443
  120.0 1.6 fusion.31
  122.4 48.8 %reduce-scatter.4.cloned.1.call-done = f32[32,64]{1,0:T(8,128)} async-done(((f32[128,64]{1,0:T(8,128)}), f32[32,64]{1,0:T(8,128)}) %reduce-scatter.4.cloned.1.call-update) | async-done | bytes 8208
  171.3 0.8 reshape.444
  172.1 0.7 copy.264
  (138 shorter events, 13.6 us)
Async XLA Ops:
  7.2 36.9 %copy-start.2 = (f32[256,3]{0,1:T(4,128)S(1)}, f32[256,3]{0,1:T(4,128)}, u32[]{:S(2)}) copy-start(f32[256,3]{0,1:T(4,128)} %param.24) | copy-start | bytes 9220
  7.9 39.9 %collective-permute-start = (f32[2,4,1,128]{3,1,2,0:T(4,128)S(1)}, f32[2,4,1,128]{3,1,2,0:T(4,128)S(1)}, u32[]{:S(2)}, u32[]{:S(2)}) collective-permute-start(f32[2,4,1,128]{3,1,2,0:T(4,128)S(1)} %pad_maximum_fusion.23), channel_id=1, source_target_pairs={{0,1},{1,2},{2,3},{3,4},{4,5},{5,6},{6,7},{8,9},{9,10},{10,11},{11... | collective-permute-start | bytes 12296 | tf_op jit(solution)/shard_map/ppermute | solution.py:41
  9.7 38.2 %collective-permute-start.1 = (f32[2,1,8,128]{3,1,2,0:T(1,128)S(1)}, f32[2,1,8,128]{3,1,2,0:T(1,128)S(1)}, u32[]{:S(2)}, u32[]{:S(2)}) collective-permute-start(f32[2,1,8,128]{3,1,2,0:T(1,128)S(1)} %pad_maximum_fusion.22), channel_id=1, source_target_pairs={{0,8},{8,16},{16,24},{24,32},{32,40},{40,48},{48,56},{56,64},{64,7... | collective-permute-start | bytes 24584 | tf_op jit(solution)/shard_map/ppermute | solution.py:41
  14.2 15.6 %collective-permute-start.10 = (f32[3,4,8,1]{3,1,2,0:T(4,128)S(1)}, f32[3,4,8,1]{3,1,2,0:T(4,128)S(1)}, u32[]{:S(2)}, u32[]{:S(2)}) collective-permute-start(f32[3,4,8,1]{3,1,2,0:T(4,128)S(1)} %get-tuple-element.88), channel_id=1, source_target_pairs={{0,128},{128,256},{256,384},{1,129},{129,257},{257,385},{2,130},{1... | collective-permute-start | bytes 1160 | tf_op jit(solution)/shard_map/ppermute | solution.py:29
  17.6 12.2 %collective-permute-start.11 = (f32[3,4,8,1]{3,1,2,0:T(4,128)S(1)}, f32[3,4,8,1]{3,1,2,0:T(4,128)S(1)}, u32[]{:S(2)}, u32[]{:S(2)}) collective-permute-start(f32[3,4,8,1]{3,1,2,0:T(4,128)S(1)} %get-tuple-element.89), channel_id=1, source_target_pairs={{128,0},{256,128},{384,256},{129,1},{257,129},{385,257},{130,2},{2... | collective-permute-start | bytes 1160 | tf_op jit(solution)/shard_map/ppermute | solution.py:31
  20.0 59.5 %collective-permute-start.2 = (f32[12,1,8,128]{3,1,2,0:T(1,128)S(1)}, f32[12,1,8,128]{3,1,2,0:T(1,128)S(1)}, u32[]{:S(2)}, u32[]{:S(2)}) collective-permute-start(f32[12,1,8,128]{3,1,2,0:T(1,128)S(1)} %get-tuple-element.62), channel_id=1, source_target_pairs={{0,8},{8,16},{16,24},{24,32},{32,40},{40,48},{48,56},{56,64},{64,7... | collective-permute-start | bytes 147464 | tf_op jit(solution)/shard_map/ppermute | solution.py:29
  30.0 6.6 %collective-permute-start.12 = (f32[3,1,8,34]{3,1,2,0:T(1,128)S(1)}, f32[3,1,8,34]{3,1,2,0:T(1,128)S(1)}, u32[]{:S(2)}, u32[]{:S(2)}) collective-permute-start(f32[3,1,8,34]{3,1,2,0:T(1,128)S(1)} %get-tuple-element.70), channel_id=1, source_target_pairs={{0,8},{8,16},{16,24},{24,32},{32,40},{40,48},{48,56},{56,64},{64,7... | collective-permute-start | bytes 9800 | tf_op jit(solution)/shard_map/ppermute | solution.py:29
  34.8 5.6 %collective-permute-start.13 = (f32[3,1,8,34]{3,1,2,0:T(1,128)S(1)}, f32[3,1,8,34]{3,1,2,0:T(1,128)S(1)}, u32[]{:S(2)}, u32[]{:S(2)}) collective-permute-start(f32[3,1,8,34]{3,1,2,0:T(1,128)S(1)} %get-tuple-element.71), channel_id=1, source_target_pairs={{8,0},{16,8},{24,16},{32,24},{40,32},{48,40},{56,48},{64,56},{72,6... | collective-permute-start | bytes 9800 | tf_op jit(solution)/shard_map/ppermute | solution.py:31
  40.4 3.7 %collective-permute-start.14 = (f32[3,6,1,34]{3,1,2,0:T(8,128)S(1)}, f32[3,6,1,34]{3,1,2,0:T(8,128)S(1)}, u32[]{:S(2)}, u32[]{:S(2)}) collective-permute-start(f32[3,6,1,34]{3,1,2,0:T(8,128)S(1)} %get-tuple-element.66), channel_id=1, source_target_pairs={{0,1},{1,2},{2,3},{3,4},{4,5},{5,6},{6,7},{8,9},{9,10},{10,11},{11... | collective-permute-start | bytes 7352 | tf_op jit(solution)/shard_map/ppermute | solution.py:29
  42.7 4.9 %collective-permute-start.15 = (f32[3,6,1,34]{3,1,2,0:T(8,128)S(1)}, f32[3,6,1,34]{3,1,2,0:T(8,128)S(1)}, u32[]{:S(2)}, u32[]{:S(2)}) collective-permute-start(f32[3,6,1,34]{3,1,2,0:T(8,128)S(1)} %get-tuple-element.67), channel_id=1, source_target_pairs={{1,0},{2,1},{3,2},{4,3},{5,4},{6,5},{7,6},{9,8},{10,9},{11,10},{12... | collective-permute-start | bytes 7352 | tf_op jit(solution)/shard_map/ppermute | solution.py:31
  44.2 35.3 %collective-permute-start.3 = (f32[12,1,8,128]{3,1,2,0:T(1,128)S(1)}, f32[12,1,8,128]{3,1,2,0:T(1,128)S(1)}, u32[]{:S(2)}, u32[]{:S(2)}) collective-permute-start(f32[12,1,8,128]{3,1,2,0:T(1,128)S(1)} %get-tuple-element.63), channel_id=1, source_target_pairs={{8,0},{16,8},{24,16},{32,24},{40,32},{48,40},{56,48},{64,56},{72,6... | collective-permute-start | bytes 147464 | tf_op jit(solution)/shard_map/ppermute | solution.py:31
  48.7 6.3 %collective-permute-start.16 = (f32[3,4,8,1]{3,1,2,0:T(4,128)S(1)}, f32[3,4,8,1]{3,1,2,0:T(4,128)S(1)}, u32[]{:S(2)}, u32[]{:S(2)}) collective-permute-start(f32[3,4,8,1]{3,1,2,0:T(4,128)S(1)} %get-tuple-element.86), channel_id=1, source_target_pairs={{0,128},{128,256},{256,384},{1,129},{129,257},{257,385},{2,130},{1... | collective-permute-start | bytes 1160 | tf_op jit(solution)/shard_map/ppermute | solution.py:29
  53.2 6.0 %collective-permute-start.17 = (f32[3,4,8,1]{3,1,2,0:T(4,128)S(1)}, f32[3,4,8,1]{3,1,2,0:T(4,128)S(1)}, u32[]{:S(2)}, u32[]{:S(2)}) collective-permute-start(f32[3,4,8,1]{3,1,2,0:T(4,128)S(1)} %get-tuple-element.87), channel_id=1, source_target_pairs={{128,0},{256,128},{384,256},{129,1},{257,129},{385,257},{130,2},{2... | collective-permute-start | bytes 1160 | tf_op jit(solution)/shard_map/ppermute | solution.py:31
  59.4 10.9 %collective-permute-start.18 = (f32[3,1,8,34]{3,1,2,0:T(1,128)S(1)}, f32[3,1,8,34]{3,1,2,0:T(1,128)S(1)}, u32[]{:S(2)}, u32[]{:S(2)}) collective-permute-start(f32[3,1,8,34]{3,1,2,0:T(1,128)S(1)} %get-tuple-element.68), channel_id=1, source_target_pairs={{0,8},{8,16},{16,24},{24,32},{32,40},{40,48},{48,56},{56,64},{64,7... | collective-permute-start | bytes 9800 | tf_op jit(solution)/shard_map/ppermute | solution.py:29
  62.0 8.3 %collective-permute-start.19 = (f32[3,1,8,34]{3,1,2,0:T(1,128)S(1)}, f32[3,1,8,34]{3,1,2,0:T(1,128)S(1)}, u32[]{:S(2)}, u32[]{:S(2)}) collective-permute-start(f32[3,1,8,34]{3,1,2,0:T(1,128)S(1)} %get-tuple-element.69), channel_id=1, source_target_pairs={{8,0},{16,8},{24,16},{32,24},{40,32},{48,40},{56,48},{64,56},{72,6... | collective-permute-start | bytes 9800 | tf_op jit(solution)/shard_map/ppermute | solution.py:31
  66.3 18.9 %all-to-all-start = ((f32[4,1,6144]{2,1,0:T(1,128)}), f32[4,1,6144]{2,1,0:T(1,128)S(1)}, u32[]{:S(2)}, u32[]{:S(2)}) async-start(f32[4,1,6144]{2,1,0:T(1,128)} %reshape.447), calls=%async_computation | async-start | bytes 196608 | tf_op jit(solution)/shard_map/all_to_all | solution.py:14
  70.4 3.4 %collective-permute-start.20 = (f32[3,6,1,34]{3,1,2,0:T(8,128)S(1)}, f32[3,6,1,34]{3,1,2,0:T(8,128)S(1)}, u32[]{:S(2)}, u32[]{:S(2)}) collective-permute-start(f32[3,6,1,34]{3,1,2,0:T(8,128)S(1)} %get-tuple-element.64), channel_id=1, source_target_pairs={{0,1},{1,2},{2,3},{3,4},{4,5},{5,6},{6,7},{8,9},{9,10},{10,11},{11... | collective-permute-start | bytes 7352 | tf_op jit(solution)/shard_map/ppermute | solution.py:29
  72.5 5.7 %collective-permute-start.21 = (f32[3,6,1,34]{3,1,2,0:T(8,128)S(1)}, f32[3,6,1,34]{3,1,2,0:T(8,128)S(1)}, u32[]{:S(2)}, u32[]{:S(2)}) collective-permute-start(f32[3,6,1,34]{3,1,2,0:T(8,128)S(1)} %get-tuple-element.65), channel_id=1, source_target_pairs={{1,0},{2,1},{3,2},{4,3},{5,4},{6,5},{7,6},{9,8},{10,9},{11,10},{12... | collective-permute-start | bytes 7352 | tf_op jit(solution)/shard_map/ppermute | solution.py:31
  79.5 12.2 %collective-permute-start.4 = (f32[12,6,1,128]{3,1,2,0:T(8,128)S(1)}, f32[12,6,1,128]{3,1,2,0:T(8,128)S(1)}, u32[]{:S(2)}, u32[]{:S(2)}) collective-permute-start(f32[12,6,1,128]{3,1,2,0:T(8,128)S(1)} %get-tuple-element.55), channel_id=1, source_target_pairs={{0,1},{1,2},{2,3},{3,4},{4,5},{5,6},{6,7},{8,9},{9,10},{10,11},{11... | collective-permute-start | bytes 110600 | tf_op jit(solution)/shard_map/ppermute | solution.py:29
  83.9 7.9 %collective-permute-start.5 = (f32[12,6,1,128]{3,1,2,0:T(8,128)S(1)}, f32[12,6,1,128]{3,1,2,0:T(8,128)S(1)}, u32[]{:S(2)}, u32[]{:S(2)}) collective-permute-start(f32[12,6,1,128]{3,1,2,0:T(8,128)S(1)} %get-tuple-element.56), channel_id=1, source_target_pairs={{1,0},{2,1},{3,2},{4,3},{5,4},{6,5},{7,6},{9,8},{10,9},{11,10},{12... | collective-permute-start | bytes 110600 | tf_op jit(solution)/shard_map/ppermute | solution.py:31
  85.2 16.1 %all-to-all-start.1 = ((f32[4,1,6144]{2,1,0:T(1,128)}), f32[4,1,6144]{2,1,0:T(1,128)S(1)}, u32[]{:S(2)}, u32[]{:S(2)}) async-start(f32[4,1,6144]{2,1,0:T(1,128)} %reshape.445), calls=%async_computation.1 | async-start | bytes 196608 | tf_op jit(solution)/shard_map/all_to_all | solution.py:14
  90.0 81.3 %reduce-scatter.4.cloned.1.call-start = ((), (), s32[]{:S(2)}) async-start(), calls=%async_computation.3 | async-start | bytes 81920
  93.4 0.9 copy-start
  93.4 1.0 copy-start.1
  94.6 7.8 %collective-permute-start.6 = (f32[12,1,8,128]{3,2,1,0:T(8,128)S(1)}, f32[12,1,8,128]{3,2,1,0:T(8,128)S(1)}, u32[]{:S(2)}, u32[]{:S(2)}) collective-permute-start(f32[12,1,8,128]{3,2,1,0:T(8,128)S(1)} %get-tuple-element.60), channel_id=1, source_target_pairs={{0,8},{8,16},{16,24},{24,32},{32,40},{40,48},{48,56},{56,64},{64,7... | collective-permute-start | bytes 147464 | tf_op jit(solution)/shard_map/ppermute | solution.py:29
  98.5 7.8 %collective-permute-start.7 = (f32[12,1,8,128]{3,2,1,0:T(8,128)S(1)}, f32[12,1,8,128]{3,2,1,0:T(8,128)S(1)}, u32[]{:S(2)}, u32[]{:S(2)}) collective-permute-start(f32[12,1,8,128]{3,2,1,0:T(8,128)S(1)} %get-tuple-element.61), channel_id=1, source_target_pairs={{8,0},{16,8},{24,16},{32,24},{40,32},{48,40},{56,48},{64,56},{72,6... | collective-permute-start | bytes 147464 | tf_op jit(solution)/shard_map/ppermute | solution.py:31
  106.3 3.6 %collective-permute-start.8 = (f32[12,6,1,128]{3,2,1,0:T(1,128)S(1)}, f32[12,6,1,128]{3,2,1,0:T(1,128)S(1)}, u32[]{:S(2)}, u32[]{:S(2)}) collective-permute-start(f32[12,6,1,128]{3,2,1,0:T(1,128)S(1)} %get-tuple-element.50), channel_id=1, source_target_pairs={{0,1},{1,2},{2,3},{3,4},{4,5},{5,6},{6,7},{8,9},{9,10},{10,11},{11... | collective-permute-start | bytes 110600 | tf_op jit(solution)/shard_map/ppermute | solution.py:29
  108.2 4.6 %collective-permute-start.9 = (f32[12,6,1,128]{3,2,1,0:T(1,128)S(1)}, f32[12,6,1,128]{3,2,1,0:T(1,128)S(1)}, u32[]{:S(2)}, u32[]{:S(2)}) collective-permute-start(f32[12,6,1,128]{3,2,1,0:T(1,128)S(1)} %get-tuple-element.51), channel_id=1, source_target_pairs={{1,0},{2,1},{3,2},{4,3},{5,4},{6,5},{7,6},{9,8},{10,9},{11,10},{12... | collective-permute-start | bytes 110600 | tf_op jit(solution)/shard_map/ppermute | solution.py:31
  117.2 0.8 copy-start.3
Sparse Core Ops, SparseCore 0:
  120.1 51.1 reduce-scatter.3
